TPU v7x, 256 devices: a whole 4x4x8 slice. The times are simulated.
256 devices in a mesh: req: 32 (over x, y, core), kv: 8 (over z).
Axes of the slice: x: 4, y: 4, z: 8, core: 2. Of those that a mesh axis runs over, the one named last changes fastest.
Arguments:
- hidden: bfloat16 [512, 1536], P('req'), may hold values from -6 to 6
- norm_gain: float32 [1536], replicated, may hold values from 0.5 to 1.5
- w_qkv: bfloat16 [1536, 3072], P(None, 'kv'), may hold values from -0.15625 to 0.15625
- w_out: bfloat16 [1536, 1536], P(None, 'kv'), may hold values from -0.15625 to 0.15625
- cache_pages: bfloat16 [6144, 2, 8, 96, 128], P('req', None, 'kv'), may hold values from -340 to 340
- lengths: int32 [512], P('req'), may hold values from 1 to 16384, as said below
- page_table: int32 [512, 128], P('req'), may hold values from 0 to 191, as said below
- occupant: int32 [512], replicated, may hold values from 0 to 511, each once
Outputs:
- mixed: bfloat16 [512, 1536], P('req', 'kv')
Inputs may be any that keep to these rules, and one draw needn't show every extreme that they name: `occupant`: every request is served at exactly one slot. Slot s holds ceil(lengths[s] / 128) pages; on every index of req the pages of its 16 slots fit its pool of 192, some pool is full, and some request has 16384 tokens. `page_table`: the first ceil(lengths[s] / 128) entries of slot s are pages of its own pool that no other slot of that pool uses; later entries are arbitrary pages of the pool.
All inputs are finite; a program needn't handle non-finite values.
Results may differ from a plain program's by a relative error of at most 0.0043.
Values may be sent and summed in bfloat16 or wider, within the bound.
No kernel may reach another device: no remote copies, remote signals or barrier semaphores. Data moves between devices by JAX's collectives and lax.ppermute only.
A program may use at most 64 MiB of HBM per device.

v0:
```python
import math
import jax
import jax.numpy as jnp
from jax import lax
from jax.sharding import PartitionSpec as P

HD = 96
PAGE = 128
MAXP = 128
GROUP = 2


def per_device(hidden, norm_gain, w_qkv, w_out, cache_pages, lengths, page_table, occupant):
    slot_count = hidden.shape[0]
    pool_size = cache_pages.shape[0]
    kv_local = cache_pages.shape[2]
    first_slot = lax.axis_index("req") * slot_count
    hidden_wide = hidden.astype(jnp.float32)
    normed = (
        hidden_wide
        * lax.rsqrt(jnp.mean(hidden_wide * hidden_wide, axis=1, keepdims=True) + 1e-05)
        * norm_gain
    ).astype(jnp.bfloat16)
    served = lax.dynamic_slice_in_dim(occupant, first_slot, slot_count)
    every_normed = lax.all_gather(normed, "req", axis=0, tiled=True)
    picked = jnp.take(every_normed, served, axis=0)
    slot_rows = jnp.dot(picked, w_qkv, preferred_element_type=jnp.float32).astype(jnp.bfloat16)
    slot_rows = slot_rows.reshape(slot_count, kv_local, GROUP + 2, HD)
    queries = slot_rows[:, :, :GROUP]
    own_key = slot_rows[:, :, GROUP]
    own_value = slot_rows[:, :, GROUP + 1]
    score_scale = 1.0 / math.sqrt(HD)
    pages_used = (lengths + PAGE - 1) // PAGE
    live_page = jnp.arange(MAXP, dtype=jnp.int32)[None, :] < pages_used[:, None]
    matches = (
        (page_table[:, :, None] == jnp.arange(pool_size, dtype=jnp.int32)[None, None, :])
        & live_page[:, :, None]
    ).astype(jnp.int32)
    owner_table = jnp.sum(matches, axis=1)
    slot_ids = jnp.arange(slot_count, dtype=jnp.int32)
    page_owner = jnp.sum(owner_table * slot_ids[:, None], axis=0)
    page_rank = jnp.sum(matches * jnp.arange(MAXP, dtype=jnp.int32)[None, :, None], axis=(0, 1))
    page_limit = jnp.sum(owner_table * lengths[:, None], axis=0)
    offsets = page_rank[:, None] * PAGE + jnp.arange(PAGE, dtype=jnp.int32)[None, :]
    token_live = offsets < page_limit[:, None]
    page_queries = jnp.take(queries, page_owner, axis=0)
    scores = (
        jnp.einsum(
            "pgjd,pgdt->pgjt", page_queries, cache_pages[:, 0], preferred_element_type=jnp.float32
        )
        * score_scale
    )
    scores = jnp.where(token_live[:, None, None, :], scores, -jnp.inf)
    page_max = jnp.max(scores, axis=-1)
    own_score = (
        jnp.sum(queries.astype(jnp.float32) * own_key.astype(jnp.float32)[:, :, None, :], axis=-1)
        * score_scale
    )
    owner_mask = owner_table > 0
    slot_max = jnp.max(jnp.where(owner_mask[:, :, None, None], page_max[None], -jnp.inf), axis=1)
    slot_max = jnp.maximum(slot_max, own_score)
    weights = jnp.exp(scores - jnp.take(slot_max, page_owner, axis=0)[..., None])
    rounded = weights.astype(jnp.bfloat16)
    page_total = jnp.sum(weights, axis=-1)
    page_numerator = jnp.einsum(
        "pgjt,pgdt->pgjd", rounded, cache_pages[:, 1], preferred_element_type=jnp.float32
    )
    own_weight = jnp.exp(own_score - slot_max)
    own_rounded = lax.optimization_barrier(own_weight.astype(jnp.bfloat16)).astype(jnp.float32)
    owner_float = owner_table.astype(jnp.float32)
    denominator = (
        jnp.einsum("sp,pgj->sgj", owner_float, page_total, precision=lax.Precision.HIGHEST)
        + own_weight
    )
    numerator = jnp.einsum(
        "sp,pgjd->sgjd", owner_float, page_numerator, precision=lax.Precision.HIGHEST
    )
    numerator = numerator + own_rounded[..., None] * own_value.astype(jnp.float32)[:, :, None, :]
    context = (numerator / denominator[..., None]).astype(jnp.bfloat16).reshape(slot_count, -1)
    gathered = lax.all_gather(context, "req", axis=0, tiled=True)
    wanted = first_slot + slot_ids
    selector = (occupant[None, :] == wanted[:, None]).astype(jnp.bfloat16)
    attended = jnp.dot(selector, gathered, preferred_element_type=jnp.float32).astype(jnp.bfloat16)
    partial_value = lax.dot_general(
        attended, w_out, (((1,), (1,)), ((), ())), preferred_element_type=jnp.float32
    )
    summed = lax.psum_scatter(partial_value, "kv", scatter_dimension=1, tiled=True)
    col_share = summed.shape[1]
    residual = lax.dynamic_slice_in_dim(hidden_wide, lax.axis_index("kv") * col_share, col_share, 1)
    return (residual + summed).astype(jnp.bfloat16)


def solution(mesh):
    return jax.shard_map(
        per_device,
        mesh=mesh,
        in_specs=(
            P("req", None),
            P(),
            P(None, "kv"),
            P(None, "kv"),
            P("req", None, "kv", None, None),
            P("req"),
            P("req", None),
            P(),
        ),
        out_specs=P("req", "kv"),
        check_vma=False,
    )
```

profile of v0, /device:TPU:2, one launch (start us, length us, event | category | flops | bytes accessed | tf_op | source)
XLA Modules:
  0.0 147.1 jit_solution(2917014156746804395)
XLA Ops:
  6.5 0.0 copy-start
  6.5 0.0 all-gather.2.cloned.1.call-start
  6.5 1.0 multiply_reduce_fusion
  7.6 1.5 %multiply_convert_fusion = bf16[16,1536]{1,0:T(8,128)(2,1)} fusion(f32[1536]{0:T(1024)} %param.9, f32[16]{0:T(128)S(1)} %add_rsqrt_fusion, bf16[16,1536]{1,0:T(8,128)(2,1)} %param.8), kind=kLoop, calls=%fused_computation.28 | loop fusion | flops 98304 | bytes 104512 | tf_op jit(solution)/shard_map/convert_element_type | solution.py:23
  9.1 0.0 all-gather.2.cloned.1.call-update
  9.1 0.0 reduce-scatter.4.cloned.1.call-start
  9.2 0.8 compare_and_fusion
  10.0 0.7 and_select_fusion
  10.6 0.1 iota_compare_fusion.1
  10.7 1.7 %select_reduce_fusion = (s32[192]{0:T(256)S(1)}, s32[16,192]{1,0:T(8,128)S(1)}) fusion(s32[16,128]{1,0:T(8,128)} %param.14, pred[16,128]{1,0:T(8,128)(4,1)S(1)} %iota_compare_fusion.1), kind=kLoop, calls=%fused_computation.10 | loop fusion | flops 2356032 | bytes 23296 | tf_op jit(solution)/shard_map/reduce_sum | solution.py:42
  12.4 0.7 multiply_reduce_fusion.2
  13.2 0.1 add_compare_fusion
  13.3 47.2 %all-gather.2.cloned.1.call-done = bf16[512,1536]{1,0:T(8,128)(2,1)} async-done(((bf16[16,1536]{1,0:T(8,128)(2,1)}), bf16[512,1536]{1,0:T(8,128)(2,1)}) %all-gather.2.cloned.1.call-update) | async-done | bytes 1572880 | tf_op jit(solution)/shard_map/all_gather | solution.py:25
  60.5 2.2 %gather_fusion = bf16[16,1536]{1,0:T(8,128)(2,1)S(1)} fusion(bf16[512,1536]{1,0:T(8,128)(2,1)} %all-gather.2.cloned.1.call-done, s32[1024]{0:T(1024)S(1)} %pad_clamp_fusion.1), kind=kCustom, calls=%fused_computation | custom fusion | bytes 98368 | tf_op jit(solution)/shard_map/jit(_take)/gather | solution.py:26
  62.7 0.0 copy-done
  62.7 0.3 convolution_convert_fusion
  63.1 0.1 reshape.230
  63.2 0.1 multiply_reduce_fusion.1
  63.3 0.1 copy.28
  63.4 0.8 gather_fusion.1
  64.2 3.8 %fusion.39 = (f32[192,2]{1,0:T(8,128)S(1)}, f32[192,2,128]{2,1,0:T(2,128)S(1)}) fusion(bf16[192,2,1,96,128]{4,3,2,1,0:T(8,128)(2,1)} %param.12, bf16[192,2,96]{2,1,0:T(2,128)(2,1)S(1)} %gather_fusion.1, pred[192]{0:T(512)(128)(4,1)S(1)} %compare_and_fusion.1, pred[192,128]{1,0:T(8,128)(4,1)S(1)} %add_compare_fusion), kind=kOutput, calls=%fused_computation.76 | convolution fusion | flops 9621120 | bytes 5015232 | tf_op jit(solution)/shard_map/pgjd,pgdt->pgjt/dot_general | solution.py:48
  68.1 0.1 copy.27
  68.2 0.1 select_reduce_fusion.1
  68.3 0.1 copy.29
  68.4 0.7 gather_fusion.2
  69.1 0.1 broadcast_select_fusion.2
  69.2 0.0 copy-start.1
  69.2 0.0 copy-start.3
  69.2 5.0 %fusion = f32[192,2,96]{2,1,0:T(2,128)S(1)} fusion(bf16[192,2,1,96,128]{4,3,2,1,0:T(8,128)(2,1)} %param.12, f32[192,2,128]{2,1,0:T(2,128)S(1)} %get-tuple-element.16, f32[192,2]{1,0:T(8,128)S(1)} %broadcast_select_fusion.2), kind=kOutput, calls=%fused_computation.3 | convolution fusion | flops 9535488 | bytes 5064192 | tf_op jit(solution)/shard_map/pgjt,pgdt->pgjd/dot_general | solution.py:65
  74.2 0.5 fusion.16
  74.7 0.0 copy-start.2
  74.8 0.3 convolution_add_fusion.1
  75.0 0.3 fusion.11
  75.3 0.1 reshape.233
  75.4 23.2 %all_gather.7 = bf16[512,192]{1,0:T(8,128)(2,1)S(1)} all-gather(bf16[16,192]{1,0:T(8,128)(2,1)S(1)} %reshape.233), channel_id=1, replica_groups=mesh['req'=32,'kv'=8] {'req'}, dimensions={0}, use_global_device_ids=true | all-gather | bytes 202752 | tf_op jit(solution)/shard_map/all_gather | solution.py:80
  98.6 0.0 copy-done.1
  98.6 0.0 copy-done.3
  98.6 1.5 %convolution_bitcast_fusion = f32[1536,16]{1,0:T(8,128)} fusion(bf16[1536,192]{0,1:T(8,128)(2,1)S(1)} %copy-done.1, bf16[512,192]{1,0:T(8,128)(2,1)S(1)} %all_gather.7, s32[512]{0:T(512)S(1)} %copy-done.3, s32[16]{0:T(128)S(1)} %iota_add_fusion), kind=kOutput, calls=%fused_computation.9 | convolution fusion | flops 12594176 | bytes 886848
  100.1 0.0 reduce-scatter.4.cloned.1.call-update
  100.1 0.0 copy-done.2
  100.2 38.5 %reduce-scatter.4.cloned.1.call-done = f32[192,16]{1,0:T(8,128)} async-done(((f32[1536,16]{1,0:T(8,128)}), f32[192,16]{1,0:T(8,128)}) %reduce-scatter.4.cloned.1.call-update) | async-done | bytes 12304
  138.6 0.9 copy.34
  139.6 0.7 add_convert_fusion
  (14 shorter events, 0.1 us)
Async XLA Ops:
  6.5 56.2 %copy-start = (bf16[1536,384]{1,0:T(8,128)(2,1)S(1)}, bf16[1536,384]{1,0:T(8,128)(2,1)}, u32[]{:S(2)}) copy-start(bf16[1536,384]{1,0:T(8,128)(2,1)} %param.10) | copy-start | bytes 3538948
  6.5 53.9 %all-gather.2.cloned.1.call-start = ((), (), s32[]{:S(2)}) async-start(), calls=%async_computation.1 | async-start | bytes 1622016 | tf_op jit(solution)/shard_map/all_gather | solution.py:25
  9.1 129.5 %reduce-scatter.4.cloned.1.call-start = ((), (), s32[]{:S(2)}) async-start(), calls=%async_computation.2 | async-start | bytes 884736
  69.2 29.5 %copy-start.1 = (bf16[1536,192]{0,1:T(8,128)(2,1)S(1)}, bf16[1536,192]{0,1:T(8,128)(2,1)}, u32[]{:S(2)}) copy-start(bf16[1536,192]{0,1:T(8,128)(2,1)} %param.11) | copy-start | bytes 1769476
  69.2 29.4 %copy-start.3 = (s32[512]{0:T(512)S(1)}, s32[512]{0:T(512)}, u32[]{:S(2)}) copy-start(s32[512]{0:T(512)} %param.15) | copy-start | bytes 6148
  74.7 25.4 %copy-start.2 = (bf16[16,1536]{1,0:T(8,128)(2,1)S(1)}, bf16[16,1536]{1,0:T(8,128)(2,1)}, u32[]{:S(2)}) copy-start(bf16[16,1536]{1,0:T(8,128)(2,1)} %param.8) | copy-start | bytes 147460
Sparse Core Ops, SparseCore 0:
  9.9 50.5 all-gather.1
  100.2 38.3 reduce-scatter.3
where the time goes:
time: 147 us
  waiting for transfers between devices  85.7 us (58%)
  blocking collectives  23.2 us (16%)
  between operations  13.6 us (9%)
  matrix products  11.2 us (8%)
  other arithmetic  8.17 us (6%)
  local copies, waits for them, and re-layouts  5.21 us (4%)
    all_gather x1, waiting for transfers between devices, per_device(): every_normed = lax.all_gather(normed, 'req', axis=0, tiled=True)  47.2 us
    unnamed x3, waiting for transfers between devices  38.5 us
    all_gather x1, blocking collectives, per_device(): gathered = lax.all_gather(context, 'req', axis=0, tiled=True)  23.2 us
    dot_general x1, matrix products, per_device(): jnp.einsum('pgjt,pgdt->pgjd', rounded, cache_pages[:, 1], preferred_eleme...  5.01 us
    dot_general x1, matrix products, per_device(): jnp.einsum('pgjd,pgdt->pgjt', page_queries, cache_pages[:, 0], preferred_...  3.85 us
  transfers between devices with their start and end apart: 2, of which 2 were waited for; matrix products, arithmetic and copies ran while one was open for 3% of the time, Pallas kernels for 0%

commit v1 on v0

--- a/solution.py
+++ b/solution.py
@@ -22,7 +22,15 @@
         * norm_gain
     ).astype(jnp.bfloat16)
     served = lax.dynamic_slice_in_dim(occupant, first_slot, slot_count)
-    every_normed = lax.all_gather(normed, "req", axis=0, tiled=True)
+
+    def treat_tasks_over_axis(shard_in):
+        slots = lax.psum(1, "req")
+        inbox = tuple((slots if dev_i == 0 else 1 for dev_i in range(shard_in.ndim)))
+        new = jnp.tile(shard_in, inbox)
+        tall = lax.all_to_all(new, "req", split_axis=0, concat_axis=0, tiled=True)
+        return tall
+
+    every_normed = treat_tasks_over_axis(normed)
     picked = jnp.take(every_normed, served, axis=0)
     slot_rows = jnp.dot(picked, w_qkv, preferred_element_type=jnp.float32).astype(jnp.bfloat16)
     slot_rows = slot_rows.reshape(slot_count, kv_local, GROUP + 2, HD)

time: 147 us -> 125 us (0.85)
  waiting for transfers between devices: 85.7 us -> 57.9 us
  starting transfers between devices: 0.04 us -> 7.8 us
  other arithmetic: 8.17 us -> 4.88 us
  blocking collectives: 23.2 us -> 24.9 us
    all_gather x1 -> x0, waiting for transfers between devices: 47.2 us -> none  [per_device(): every_normed = lax.all_gather(normed, 'req', axis=0, tiled=True)]
    all_to_all x0 -> x1, waiting for transfers between devices: none -> 18.6 us  [treat_tasks_over_axis(): tall = lax.all_to_all(new, 'req', split_axis=0, concat_axis=0, tiled=True)]
    all_to_all x0 -> x1, starting transfers between devices: none -> 7.75 us  [treat_tasks_over_axis(): tall = lax.all_to_all(new, 'req', split_axis=0, concat_axis=0, tiled=True)]
    gather x1, local copies, waits for them, and re-layouts: 2.25 us -> 0.59 us  [per_device(): picked = jnp.take(every_normed, served, axis=0)]
    all_gather x1, blocking collectives: 23.2 us -> 24.9 us  [per_device(): gathered = lax.all_gather(context, 'req', axis=0, tiled=True)]
    unnamed x3 -> x2, waiting for transfers between devices: 38.5 us -> 39.3 us
  transfers between devices with their start and end apart: 2 -> 2, of which waited for: 2 -> 2; matrix products, arithmetic and copies ran while one was open for 3% -> 1% of each run, Pallas kernels for 0% -> 0%
where the time goes in v1:
time: 125 us
  waiting for transfers between devices  57.9 us (46%)
  blocking collectives  24.9 us (20%)
  between operations  13.6 us (11%)
  matrix products  11.2 us (9%)
  starting transfers between devices  7.8 us (6%)
  local copies, waits for them, and re-layouts  4.89 us (4%)
  other arithmetic  4.88 us (4%)
    unnamed x2, waiting for transfers between devices  39.3 us
    all_gather x1, blocking collectives, per_device(): gathered = lax.all_gather(context, 'req', axis=0, tiled=True)  24.9 us
    all_to_all x1, waiting for transfers between devices, treat_tasks_over_axis(): tall = lax.all_to_all(new, 'req', split_axis=0, concat_axis=0, tiled=True)  18.6 us
    all_to_all x1, starting transfers between devices, treat_tasks_over_axis(): tall = lax.all_to_all(new, 'req', split_axis=0, concat_axis=0, tiled=True)  7.75 us
    dot_general x1, matrix products, per_device(): jnp.einsum('pgjt,pgdt->pgjd', rounded, cache_pages[:, 1], preferred_eleme...  5.01 us
    dot_general x1, matrix products, per_device(): jnp.einsum('pgjd,pgdt->pgjt', page_queries, cache_pages[:, 0], preferred_...  3.84 us
  transfers between devices with their start and end apart: 2, of which 2 were waited for; matrix products, arithmetic and copies ran while one was open for 1% of the time, Pallas kernels for 0%

profile of v1, /device:TPU:2, one launch (start us, length us, event | category | flops | bytes accessed | tf_op | source)
XLA Modules:
  0.0 125.1 jit_solution(12680022186596960200)
XLA Ops:
  6.5 0.0 copy-start
  6.5 1.0 multiply_reduce_fusion
  7.6 0.9 multiply_convert_fusion
  8.5 1.3 %tile.2 = bf16[32,16,1536]{2,1,0:T(8,128)(2,1)} broadcast(bf16[16,1536]{1,0:T(8,128)(2,1)S(1)} %multiply_convert_fusion), dimensions={1,2} | broadcast | bytes 1622016 | tf_op jit(solution)/shard_map/tile | solution.py:29
  9.8 0.0 copy-start.4
  9.8 0.0 copy-start.5
  9.8 0.0 copy-start.3
  9.8 7.8 %all-to-all-start = ((bf16[32,16,1536]{2,1,0:T(8,128)(2,1)}), bf16[32,16,1536]{2,1,0:T(8,128)(2,1)S(1)}, u32[]{:S(2)}, u32[]{:S(2)}) async-start(bf16[32,16,1536]{2,1,0:T(8,128)(2,1)} %tile.2), calls=%async_computation | async-start | bytes 3145728 | tf_op jit(solution)/shard_map/all_to_all | solution.py:30
  17.6 0.0 reduce-scatter.4.cloned.1.call-start
  17.6 0.0 copy-done.4
  17.6 0.1 compare_and_fusion
  17.7 0.0 copy-done.5
  17.8 0.1 iota_compare_fusion.1
  17.8 0.0 copy-done.3
  17.8 1.0 select_reduce_fusion
  18.8 0.1 multiply_reduce_fusion.2
  19.0 0.1 add_compare_fusion
  19.1 18.6 %all-to-all-done = bf16[32,16,1536]{2,1,0:T(8,128)(2,1)S(1)} async-done(((bf16[32,16,1536]{2,1,0:T(8,128)(2,1)}), bf16[32,16,1536]{2,1,0:T(8,128)(2,1)S(1)}, u32[]{:S(2)}, u32[]{:S(2)}) %all-to-all-start) | async-done | bytes 1572896 | tf_op jit(solution)/shard_map/all_to_all | solution.py:30
  37.7 0.6 gather_fusion
  38.3 0.0 copy-done
  38.3 0.3 convolution_convert_fusion
  38.6 0.1 reshape.237
  38.8 0.1 multiply_reduce_fusion.1
  38.9 0.1 copy.28
  38.9 0.8 gather_fusion.1
  39.8 3.8 %fusion.39 = (f32[192,2]{1,0:T(8,128)S(1)}, f32[192,2,128]{2,1,0:T(2,128)S(1)}) fusion(bf16[192,2,1,96,128]{4,3,2,1,0:T(8,128)(2,1)} %param.12, bf16[192,2,96]{2,1,0:T(2,128)(2,1)S(1)} %gather_fusion.1, pred[192]{0:T(512)(128)(4,1)S(1)} %compare_and_fusion.1, pred[192,128]{1,0:T(8,128)(4,1)S(1)} %add_compare_fusion), kind=kOutput, calls=%fused_computation.76 | convolution fusion | flops 9621120 | bytes 5015232 | tf_op jit(solution)/shard_map/pgjd,pgdt->pgjt/dot_general | solution.py:56
  43.6 0.1 copy.27
  43.7 0.1 select_reduce_fusion.1
  43.8 0.1 copy.29
  43.9 0.7 gather_fusion.2
  44.6 0.1 broadcast_select_fusion.2
  44.7 0.0 copy-start.1
  44.7 5.0 %fusion = f32[192,2,96]{2,1,0:T(2,128)S(1)} fusion(bf16[192,2,1,96,128]{4,3,2,1,0:T(8,128)(2,1)} %param.12, f32[192,2,128]{2,1,0:T(2,128)S(1)} %get-tuple-element.16, f32[192,2]{1,0:T(8,128)S(1)} %broadcast_select_fusion.2), kind=kOutput, calls=%fused_computation.3 | convolution fusion | flops 9535488 | bytes 5064192 | tf_op jit(solution)/shard_map/pgjt,pgdt->pgjd/dot_general | solution.py:73
  49.7 0.5 fusion.16
  50.3 0.0 copy-start.2
  50.3 0.3 convolution_add_fusion.1
  50.5 0.3 fusion.11
  50.8 0.1 reshape.240
  50.9 24.9 %all_gather.3 = bf16[512,192]{1,0:T(8,128)(2,1)S(1)} all-gather(bf16[16,192]{1,0:T(8,128)(2,1)S(1)} %reshape.240), channel_id=1, replica_groups=mesh['req'=32,'kv'=8] {'req'}, dimensions={0}, use_global_device_ids=true | all-gather | bytes 202752 | tf_op jit(solution)/shard_map/all_gather | solution.py:88
  75.8 0.0 copy-done.1
  75.8 1.5 %convolution_bitcast_fusion = f32[1536,16]{1,0:T(8,128)} fusion(bf16[1536,192]{0,1:T(8,128)(2,1)S(1)} %copy-done.1, bf16[512,192]{1,0:T(8,128)(2,1)S(1)} %all_gather.3, s32[512]{0:T(512)S(1)} %copy-done.4, s32[16]{0:T(128)S(1)} %iota_add_fusion), kind=kOutput, calls=%fused_computation.9 | convolution fusion | flops 12594176 | bytes 886848
  77.3 0.0 reduce-scatter.4.cloned.1.call-update
  77.3 0.0 copy-done.2
  77.3 39.3 %reduce-scatter.4.cloned.1.call-done = f32[192,16]{1,0:T(8,128)} async-done(((f32[1536,16]{1,0:T(8,128)}), f32[192,16]{1,0:T(8,128)}) %reduce-scatter.4.cloned.1.call-update) | async-done | bytes 12304
  116.7 0.9 copy.34
  117.6 0.7 add_convert_fusion
  (15 shorter events, 0.1 us)
Async XLA Ops:
  6.5 31.8 %copy-start = (bf16[1536,384]{1,0:T(8,128)(2,1)S(1)}, bf16[1536,384]{1,0:T(8,128)(2,1)}, u32[]{:S(2)}) copy-start(bf16[1536,384]{1,0:T(8,128)(2,1)} %param.10) | copy-start | bytes 3538948
  9.8 7.8 %copy-start.4 = (s32[512]{0:T(512)S(1)}, s32[512]{0:T(512)}, u32[]{:S(2)}) copy-start(s32[512]{0:T(512)} %param.15) | copy-start | bytes 6148
  9.8 7.9 %copy-start.5 = (s32[16]{0:T(128)S(1)}, s32[16]{0:T(128)}, u32[]{:S(2)}) copy-start(s32[16]{0:T(128)} %param.13) | copy-start | bytes 196
  9.8 8.0 %copy-start.3 = (s32[16,128]{1,0:T(8,128)S(1)}, s32[16,128]{1,0:T(8,128)}, u32[]{:S(2)}) copy-start(s32[16,128]{1,0:T(8,128)} %param.14) | copy-start | bytes 24580
  9.8 27.9 %all-to-all-start = ((bf16[32,16,1536]{2,1,0:T(8,128)(2,1)}), bf16[32,16,1536]{2,1,0:T(8,128)(2,1)S(1)}, u32[]{:S(2)}, u32[]{:S(2)}) async-start(bf16[32,16,1536]{2,1,0:T(8,128)(2,1)} %tile.2), calls=%async_computation | async-start | bytes 3145728 | tf_op jit(solution)/shard_map/all_to_all | solution.py:30
  17.6 99.1 %reduce-scatter.4.cloned.1.call-start = ((), (), s32[]{:S(2)}) async-start(), calls=%async_computation.2 | async-start | bytes 884736
  44.7 31.1 %copy-start.1 = (bf16[1536,192]{0,1:T(8,128)(2,1)S(1)}, bf16[1536,192]{0,1:T(8,128)(2,1)}, u32[]{:S(2)}) copy-start(bf16[1536,192]{0,1:T(8,128)(2,1)} %param.11) | copy-start | bytes 1769476
  50.3 27.0 %copy-start.2 = (bf16[16,1536]{1,0:T(8,128)(2,1)S(1)}, bf16[16,1536]{1,0:T(8,128)(2,1)}, u32[]{:S(2)}) copy-start(bf16[16,1536]{1,0:T(8,128)(2,1)} %param.8) | copy-start | bytes 147460
Sparse Core Ops, SparseCore 0:
  77.4 39.1 reduce-scatter.3
